TPU v7x, 32 devices: a whole 2x2x4 slice. The times are simulated.
32 devices in a mesh: grp: 2 (over x), date: 16 (over z, y, core).
Axes of the slice: x: 2, y: 2, z: 4, core: 2. Of those that a mesh axis runs over, the one named last changes fastest.
Arguments:
- slc: bfloat16 [16, 2, 128, 2048], P('date', None, 'grp'), parts along dimension 2, may hold values from -6 to 6
- pairs: int32 [64, 2], replicated, may hold values from 0 to 15, as said below
- inverse: bfloat16 [15, 64], replicated, may hold values from -6 to 6
Outputs:
- series: float32 [15, 32, 128], P(None, ('grp', 'date')), parts along dimension 1
There are 2 independent parts, one for each index of `grp`. A program takes and returns all parts, laid end to end along the dimension named above; an argument that names none is the same for every part. Nothing has to cross between parts.
Inputs may be any that keep to these rules, and one draw needn't show every extreme that they name: pairs[p,0] < pairs[p,1] for every pair.
All inputs are finite; a program needn't handle non-finite values.
Results may differ from a plain program's by a relative error of at most 0.0003.
Values may be sent and summed in bfloat16 or wider, within the bound.
No kernel may reach another device: no remote copies, remote signals or barrier semaphores. Data moves between devices by JAX's collectives and lax.ppermute only.
A program may use at most 128 MiB of HBM per device.

v0:
```python
import jax
import jax.numpy as jnp
from jax import lax
from jax.sharding import PartitionSpec as P

LOOK_R = 4
LOOK_C = 16


def coherence(first, second):
    first = first.astype(jnp.float32)
    second = second.astype(jnp.float32)
    cross = first[:, 1] * second[:, 0] - first[:, 0] * second[:, 1]
    power_ref = first[:, 0] * first[:, 0] + first[:, 1] * first[:, 1]
    power_sec = second[:, 0] * second[:, 0] + second[:, 1] * second[:, 1]
    stacked = jnp.stack([cross, power_ref, power_sec])
    three, count, rows, cols = stacked.shape
    rowsum = stacked.reshape(three, count, rows // LOOK_R, LOOK_R, cols).sum(axis=3)
    window = (jnp.arange(cols)[:, None] // LOOK_C == jnp.arange(cols // LOOK_C)[None, :]).astype(
        jnp.float32
    )
    looked = jnp.dot(rowsum, window, precision=lax.Precision.HIGHEST)
    return looked[0] / jnp.sqrt(looked[1] * looked[2] + 1e-06)


def invert(inverse, proxy):
    return jnp.einsum(
        "sp,pxy->sxy", inverse.astype(jnp.float32), proxy, precision=lax.Precision.HIGHEST
    )


def per_device(slc, pairs, inverse):
    stripes = lax.all_to_all(slc, "date", split_axis=2, concat_axis=0, tiled=True)
    first = jnp.take(stripes, pairs[:, 0], axis=0)
    second = jnp.take(stripes, pairs[:, 1], axis=0)
    proxy = coherence(first, second)
    return invert(inverse, proxy)


def solution(mesh):
    in_specs = (P("date", None, "grp", None), P(), P())
    out_specs = P(None, ("grp", "date"), None)
    return jax.shard_map(
        per_device, mesh=mesh, in_specs=in_specs, out_specs=out_specs, check_vma=False
    )
```

profile of v0, /device:TPU:0, one launch (start us, length us, event | category | flops | bytes accessed | tf_op | source)
XLA Modules:
  0.0 41.9 jit_solution(5127418015980830979)
XLA Ops:
  0.0 0.0 copy-start
  0.0 0.0 copy-start.1
  0.0 2.4 %copy.26 = bf16[1,2,64,2048]{3,1,0,2:T(2,128)(2,1)} copy(bf16[1,2,64,2048]{3,2,1,0:T(8,128)(2,1)} %param.5) | data formatting | bytes 1048576 | tf_op args[0]
  2.4 7.4 %all-to-all-start = ((bf16[1,2,64,2048]{3,1,0,2:T(2,128)(2,1)}), bf16[1,2,64,2048]{3,1,0,2:T(2,128)(2,1)S(1)}, u32[]{:S(2)}, u32[]{:S(2)}) async-start(bf16[1,2,64,2048]{3,1,0,2:T(2,128)(2,1)} %copy.26), calls=%async_computation | async-start | bytes 1048576 | tf_op jit(solution)/shard_map/all_to_all | solution.py:33
  9.8 0.0 copy-done.1
  9.9 14.2 %all-to-all-done = bf16[1,2,64,2048]{3,1,0,2:T(2,128)(2,1)S(1)} async-done(((bf16[1,2,64,2048]{3,1,0,2:T(2,128)(2,1)}), bf16[1,2,64,2048]{3,1,0,2:T(2,128)(2,1)S(1)}, u32[]{:S(2)}, u32[]{:S(2)}) %all-to-all-start) | async-done | bytes 524320 | tf_op jit(solution)/shard_map/all_to_all | solution.py:33
  24.1 0.3 copy.38
  24.4 2.4 %gather_fusion = bf16[64,2,4,2048]{3,2,1,0:T(4,128)(2,1)S(1)} fusion(bf16[16,2,4,2048]{3,2,1,0:T(4,128)(2,1)S(1)} %bitcast.30, s32[1024]{0:T(1024)S(1)} %pad_clamp_fusion.1), kind=kCustom, calls=%fused_computation.clone | custom fusion | bytes 4194560 | tf_op jit(solution)/shard_map/jit(_take)/gather | solution.py:34
  26.7 3.6 %gather_fusion.1 = bf16[64,2,4,2048]{3,2,1,0:T(4,128)(2,1)} fusion(bf16[16,2,4,2048]{3,2,1,0:T(4,128)(2,1)S(1)} %bitcast.31, s32[1024]{0:T(1024)S(1)} %pad_clamp_fusion), kind=kCustom, calls=%fused_computation.1.clone | custom fusion | bytes 4194560 | tf_op jit(solution)/shard_map/jit(_take)/gather | solution.py:35
  30.3 7.5 %fusion = (f32[64,2,4,2048]{3,0,2,1:T(8,128)S(1)}, f32[64,2,4,2048]{3,0,2,1:T(8,128)S(1)}) fusion(bf16[64,2,4,2048]{3,2,1,0:T(4,128)(2,1)} %gather_fusion.1, pred[64]{0:T(512)(128)(4,1)S(1)} %get-tuple-element.13, bf16[64,2,4,2048]{3,2,1,0:T(4,128)(2,1)S(1)} %gather_fusion, pred[64]{0:T(512)(128)(4,1)S(1)} %get-tuple-element.6), kind=kLoop, calls=%fused_computation.4 | loop fusion | flops 4194304 | bytes 12583040 | tf_op jit(solution)/shard_map/convert_element_type | solution.py:12
  37.8 1.6 %subtract_bitcast_fusion = (f32[1,64,4,2048]{3,1,2,0:T(8,128)S(1)}, f32[1,64,4,2048]{3,1,2,0:T(8,128)S(1)}, f32[1,64,4,2048]{3,1,2,0:T(8,128)S(1)}) fusion(f32[64,2,4,2048]{3,0,2,1:T(8,128)S(1)} %get-tuple-element.15, f32[64,2,4,2048]{3,0,2,1:T(8,128)S(1)} %get-tuple-element.16), kind=kLoop, calls=%fused_computation.9 | loop fusion | flops 4718592 | bytes 14680064 | tf_op jit(solution)/shard_map/sub | solution.py:13
  39.5 0.7 %maximum_reduce_fusion = f32[3,64,2048]{2,1,0:T(8,128)S(1)} fusion(f32[1,64,4,2048]{3,1,2,0:T(8,128)S(1)} %get-tuple-element.12, f32[1,64,4,2048]{3,1,2,0:T(8,128)S(1)} %get-tuple-element.11, f32[1,64,4,2048]{3,1,2,0:T(8,128)S(1)} %get-tuple-element.10), kind=kLoop, calls=%fused_computation.2 | loop fusion | flops 4325376 | bytes 7864320 | tf_op jit(solution)/shard_map/reduce_sum | solution.py:18
  40.1 1.0 %fusion.3 = f32[3,64,128]{2,1,0:T(8,128)S(1)} fusion(f32[3,64,2048]{2,1,0:T(8,128)S(1)} %maximum_reduce_fusion, s32[2048]{0:T(1024)S(1)} %add_select_fusion), kind=kOutput, calls=%fused_computation.13 | convolution fusion | flops 604241920 | bytes 1679360 | tf_op jit(solution)/shard_map/dot_general | solution.py:22
  41.2 0.0 copy-done
  41.2 0.1 convolution_bitcast_fusion
  41.3 0.6 %copy.30 = f32[15,1,128]{2,1,0:T(1,128)} copy(f32[15,1,128]{2,0,1:T(8,128)S(1)} %convolution_bitcast_fusion) | data formatting | bytes 15360 | tf_op jit(solution)/shard_map/sp,pxy->sxy/dot_general | solution.py:27
  (4 shorter events, 0.0 us)
Async XLA Ops:
  0.0 41.2 %copy-start = (bf16[15,64]{1,0:T(8,128)(2,1)S(1)}, bf16[15,64]{1,0:T(8,128)(2,1)}, u32[]{:S(2)}) copy-start(bf16[15,64]{1,0:T(8,128)(2,1)} %param.7) | copy-start | bytes 5764
  0.0 9.8 %copy-start.1 = (s32[64,2]{0,1:T(2,128)S(1)}, s32[64,2]{0,1:T(2,128)}, u32[]{:S(2)}) copy-start(s32[64,2]{0,1:T(2,128)} %param.6) | copy-start | bytes 1540
  2.4 21.7 %all-to-all-start = ((bf16[1,2,64,2048]{3,1,0,2:T(2,128)(2,1)}), bf16[1,2,64,2048]{3,1,0,2:T(2,128)(2,1)S(1)}, u32[]{:S(2)}, u32[]{:S(2)}) async-start(bf16[1,2,64,2048]{3,1,0,2:T(2,128)(2,1)} %copy.26), calls=%async_computation | async-start | bytes 1048576 | tf_op jit(solution)/shard_map/all_to_all | solution.py:33
where the time goes:
time: 42.2 us; the launch traced here: 41.9 us
  waiting for transfers between devices  14.2 us (34%)
  other arithmetic  9.83 us (23%)
  local copies, waits for them, and re-layouts  9.23 us (22%)
  starting transfers between devices  7.41 us (18%)
  matrix products  1.16 us (3%)
    all_to_all x1, waiting for transfers between devices, per_device(): lax.all_to_all(slc, 'date', split_axis=2, concat_axis=0, tiled=True)  14.2 us
    convert_element_type x1, other arithmetic, coherence(): second = second.astype(jnp.float32)  7.53 us
    all_to_all x1, starting transfers between devices, per_device(): lax.all_to_all(slc, 'date', split_axis=2, concat_axis=0, tiled=True)  7.41 us
    gather x1, local copies, waits for them, and re-layouts, per_device(): second = jnp.take(stripes, pairs[:, 1], axis=0)  3.56 us
    unnamed x5, local copies, waits for them, and re-layouts  2.41 us
    gather x1, local copies, waits for them, and re-layouts, per_device(): first = jnp.take(stripes, pairs[:, 0], axis=0)  2.36 us
    sub x1, other arithmetic, coherence(): cross = first[:, 1] * second[:, 0] - first[:, 0] * second[:, 1]  1.62 us
    dot_general x1, matrix products, coherence(): looked = jnp.dot(rowsum, window, precision=lax.Precision.HIGHEST)  1.03 us
  transfers between devices with their start and end apart: 1, of which 1 were waited for; matrix products, arithmetic and copies ran while one was open for 0% of the time, Pallas kernels for 0%

commit v1 on v0

--- a/solution.py
+++ b/solution.py
@@ -2,9 +2,33 @@
 import jax.numpy as jnp
 from jax import lax
 from jax.sharding import PartitionSpec as P
+from jax.lax import axis_index, axis_size, ppermute
 
 LOOK_R = 4
 LOOK_C = 16
+
+
+def step_on_object(array_here, dim_at, frame):
+    upper = array_here.shape
+    v_now = array_here.reshape(*upper[:dim_at], frame, upper[dim_at] // frame, *upper[dim_at + 1 :])
+    return jnp.moveaxis(v_now, dim_at, 0)
+
+
+def cover_the_body(block_in, d0):
+    block_in = jnp.moveaxis(block_in, 0, d0)
+    s_next = block_in.shape
+    return block_in.reshape(*s_next[:d0], s_next[d0] * s_next[d0 + 1], *s_next[d0 + 2 :])
+
+
+def pair_things(a0, row_axis, incoming_x, chunk):
+    finding, b_next = (axis_size(row_axis), axis_index(row_axis))
+    b_now = step_on_object(a0, incoming_x, finding)
+    xs_all = [b_now[b_next]]
+    for rr in range(1, finding):
+        w1 = b_now[b_next ^ rr]
+        xs_all.append(ppermute(w1, row_axis, [(dd, dd ^ rr) for dd in range(finding)]))
+    b_now = jnp.stack(xs_all, axis=0)[b_next ^ jnp.arange(finding)]
+    return cover_the_body(b_now, chunk)
 
 
 def coherence(first, second):
@@ -30,7 +54,7 @@
 
 
 def per_device(slc, pairs, inverse):
-    stripes = lax.all_to_all(slc, "date", split_axis=2, concat_axis=0, tiled=True)
+    stripes = pair_things(slc, "date", 2, 0)
     first = jnp.take(stripes, pairs[:, 0], axis=0)
     second = jnp.take(stripes, pairs[:, 1], axis=0)
     proxy = coherence(first, second)

time: 42.2 us -> 48.5 us (1.15)
  starting transfers between devices: 7.41 us -> 22.7 us
  waiting for transfers between devices: 14.2 us -> 5.89 us
  other arithmetic: 9.83 us -> 8.77 us
    ppermute x0 -> x15, starting transfers between devices: none -> 22.7 us  [pair_things(): ppermute(w1, row_axis, [(dd, dd ^ rr) for dd in range(finding)])]
    all_to_all x1 -> x0, waiting for transfers between devices: 14.2 us -> none  [per_device(): lax.all_to_all(slc, 'date', split_axis=2, concat_axis=0, tiled=True)]
    all_to_all x1 -> x0, starting transfers between devices: 7.41 us -> none  [per_device(): lax.all_to_all(slc, 'date', split_axis=2, concat_axis=0, tiled=True)]
    ppermute x0 -> x15, waiting for transfers between devices: none -> 5.89 us  [pair_things(): ppermute(w1, row_axis, [(dd, dd ^ rr) for dd in range(finding)])]
    convert_element_type x1, other arithmetic: 7.53 us -> 2.44 us  [coherence(): second = second.astype(jnp.float32)]
    convert_element_type x0 -> x1, other arithmetic: none -> 4.03 us  [coherence(): first = first.astype(jnp.float32)]
    unnamed x5 -> x19, local copies, waits for them, and re-layouts: 2.41 us -> 0.33 us
    reshape x0 -> x1, local copies, waits for them, and re-layouts: none -> 1.26 us  [step_on_object(): array_here.reshape(*upper[:dim_at], frame, upper[dim_at] // frame, *upper...]
  transfers between devices with their start and end apart: 1 -> 15, of which waited for: 1 -> 3; matrix products, arithmetic and copies ran while one was open for 0% -> 1% of each run, Pallas kernels for 0% -> 0%
where the time goes in v1:
time: 48.5 us; the launch traced here: 48.3 us
  starting transfers between devices  22.7 us (47%)
  local copies, waits for them, and re-layouts  9.45 us (19%)
  other arithmetic  8.77 us (18%)
  waiting for transfers between devices  5.89 us (12%)
  matrix products  1.16 us (2%)
    ppermute x15, starting transfers between devices, pair_things(): ppermute(w1, row_axis, [(dd, dd ^ rr) for dd in range(finding)])  22.7 us
    ppermute x15, waiting for transfers between devices, pair_things(): ppermute(w1, row_axis, [(dd, dd ^ rr) for dd in range(finding)])  5.89 us
    convert_element_type x1, other arithmetic, coherence(): first = first.astype(jnp.float32)  4.03 us
    gather x1, local copies, waits for them, and re-layouts, per_device(): first = jnp.take(stripes, pairs[:, 0], axis=0)  3.57 us
    convert_element_type x1, other arithmetic, coherence(): second = second.astype(jnp.float32)  2.44 us
    gather x1, local copies, waits for them, and re-layouts, per_device(): second = jnp.take(stripes, pairs[:, 1], axis=0)  2.36 us
    sub x1, other arithmetic, coherence(): cross = first[:, 1] * second[:, 0] - first[:, 0] * second[:, 1]  1.62 us
    reshape x1, local copies, waits for them, and re-layouts, step_on_object(): array_here.reshape(*upper[:dim_at], frame, upper[dim_at] // frame, *upper...  1.26 us
  transfers between devices with their start and end apart: 15, of which 3 were waited for; matrix products, arithmetic and copies ran while one was open for 1% of the time, Pallas kernels for 0%

profile of v1, /device:TPU:0, one launch (start us, length us, event | category | flops | bytes accessed | tf_op | source)
XLA Modules:
  0.0 48.3 jit_solution(15089032739558214178)
XLA Ops:
  0.0 0.0 copy-start
  0.0 0.0 copy-start.1
  0.0 1.3 %reshape.218 = bf16[1,2,16,4,2048]{4,3,2,1,0:T(4,128)(2,1)S(1)} reshape(bf16[1,2,64,2048]{3,2,1,0:T(8,128)(2,1)} %param.5) | data formatting | bytes 1048576 | tf_op jit(solution)/shard_map/reshape | solution.py:13
  1.4 0.3 dynamic-slice_bitcast_fusion
  1.6 0.6 %collective-permute-start = (bf16[1,2,4,2048]{3,2,1,0:T(4,128)(2,1)S(1)}, bf16[1,2,4,2048]{3,2,1,0:T(4,128)(2,1)S(1)}, u32[]{:S(2)}, u32[]{:S(2)}) collective-permute-start(bf16[1,2,4,2048]{3,2,1,0:T(4,128)(2,1)S(1)} %get-tuple-element.27), channel_id=1, source_target_pairs={{0,1},{1,0},{2,3},{3,2},{4,5},{5,4},{6,7},{7,6},{8,9},{9,8},{10,11... | collective-permute-start | bytes 98312 | tf_op jit(solution)/shard_map/ppermute | solution.py:29
  2.2 2.6 %collective-permute-start.1 = (bf16[1,2,4,2048]{3,2,1,0:T(4,128)(2,1)S(1)}, bf16[1,2,4,2048]{3,2,1,0:T(4,128)(2,1)S(1)}, u32[]{:S(2)}, u32[]{:S(2)}) collective-permute-start(bf16[1,2,4,2048]{3,2,1,0:T(4,128)(2,1)S(1)} %get-tuple-element.26), channel_id=1, source_target_pairs={{0,2},{1,3},{2,0},{3,1},{4,6},{5,7},{6,4},{7,5},{8,10},{9,11},{10,... | collective-permute-start | bytes 98312 | tf_op jit(solution)/shard_map/ppermute | solution.py:29
  4.8 0.0 collective-permute-start.2
  4.8 1.8 %collective-permute-start.3 = (bf16[1,2,4,2048]{3,2,1,0:T(4,128)(2,1)S(1)}, bf16[1,2,4,2048]{3,2,1,0:T(4,128)(2,1)S(1)}, u32[]{:S(2)}, u32[]{:S(2)}) collective-permute-start(bf16[1,2,4,2048]{3,2,1,0:T(4,128)(2,1)S(1)} %get-tuple-element.24), channel_id=1, source_target_pairs={{0,4},{1,5},{2,6},{3,7},{4,0},{5,1},{6,2},{7,3},{8,12},{9,13},{10,... | collective-permute-start | bytes 98312 | tf_op jit(solution)/shard_map/ppermute | solution.py:29
  6.6 0.0 collective-permute-start.4
  6.7 0.0 copy-done.1
  6.7 0.0 collective-permute-done
  6.7 2.7 %collective-permute-start.5 = (bf16[1,2,4,2048]{3,2,1,0:T(4,128)(2,1)S(1)}, bf16[1,2,4,2048]{3,2,1,0:T(4,128)(2,1)S(1)}, u32[]{:S(2)}, u32[]{:S(2)}) collective-permute-start(bf16[1,2,4,2048]{3,2,1,0:T(4,128)(2,1)S(1)} %get-tuple-element.22), channel_id=1, source_target_pairs={{0,6},{1,7},{2,4},{3,5},{4,2},{5,3},{6,0},{7,1},{8,14},{9,15},{10,... | collective-permute-start | bytes 98312 | tf_op jit(solution)/shard_map/ppermute | solution.py:29
  9.5 0.0 collective-permute-done.1
  9.5 0.1 collective-permute-start.6
  9.6 0.0 collective-permute-done.2
  9.6 2.7 %collective-permute-start.7 = (bf16[1,2,4,2048]{3,2,1,0:T(4,128)(2,1)S(1)}, bf16[1,2,4,2048]{3,2,1,0:T(4,128)(2,1)S(1)}, u32[]{:S(2)}, u32[]{:S(2)}) collective-permute-start(bf16[1,2,4,2048]{3,2,1,0:T(4,128)(2,1)S(1)} %get-tuple-element.20), channel_id=1, source_target_pairs={{0,8},{1,9},{2,10},{3,11},{4,12},{5,13},{6,14},{7,15},{8,0},{9,1},... | collective-permute-start | bytes 98312 | tf_op jit(solution)/shard_map/ppermute | solution.py:29
  12.4 0.0 collective-permute-done.3
  12.4 0.1 collective-permute-start.8
  12.6 0.0 collective-permute-done.4
  12.6 3.6 %collective-permute-start.9 = (bf16[1,2,4,2048]{3,2,1,0:T(4,128)(2,1)S(1)}, bf16[1,2,4,2048]{3,2,1,0:T(4,128)(2,1)S(1)}, u32[]{:S(2)}, u32[]{:S(2)}) collective-permute-start(bf16[1,2,4,2048]{3,2,1,0:T(4,128)(2,1)S(1)} %get-tuple-element.18), channel_id=1, source_target_pairs={{0,10},{1,11},{2,8},{3,9},{4,14},{5,15},{6,12},{7,13},{8,2},{9,3},... | collective-permute-start | bytes 98312 | tf_op jit(solution)/shard_map/ppermute | solution.py:29
  16.2 0.0 collective-permute-done.5
  16.2 0.1 collective-permute-start.10
  16.3 0.0 collective-permute-done.6
  16.3 3.6 %collective-permute-start.11 = (bf16[1,2,4,2048]{3,2,1,0:T(4,128)(2,1)S(1)}, bf16[1,2,4,2048]{3,2,1,0:T(4,128)(2,1)S(1)}, u32[]{:S(2)}, u32[]{:S(2)}) collective-permute-start(bf16[1,2,4,2048]{3,2,1,0:T(4,128)(2,1)S(1)} %get-tuple-element.16), channel_id=1, source_target_pairs={{0,12},{1,13},{2,14},{3,15},{4,8},{5,9},{6,10},{7,11},{8,4},{9,5},... | collective-permute-start | bytes 98312 | tf_op jit(solution)/shard_map/ppermute | solution.py:29
  20.0 0.0 collective-permute-done.7
  20.0 0.1 collective-permute-start.12
  20.1 0.0 collective-permute-done.8
  20.1 4.5 %collective-permute-start.13 = (bf16[1,2,4,2048]{3,2,1,0:T(4,128)(2,1)S(1)}, bf16[1,2,4,2048]{3,2,1,0:T(4,128)(2,1)S(1)}, u32[]{:S(2)}, u32[]{:S(2)}) collective-permute-start(bf16[1,2,4,2048]{3,2,1,0:T(4,128)(2,1)S(1)} %get-tuple-element.14), channel_id=1, source_target_pairs={{0,14},{1,15},{2,12},{3,13},{4,10},{5,11},{6,8},{7,9},{8,6},{9,7},... | collective-permute-start | bytes 98312 | tf_op jit(solution)/shard_map/ppermute | solution.py:29
  24.7 0.0 collective-permute-done.9
  24.7 0.1 collective-permute-start.14
  24.8 0.0 collective-permute-done.10
  24.8 0.0 collective-permute-done.11
  24.9 0.5 collective-permute-done.12
  25.4 2.0 %collective-permute-done.13 = bf16[1,2,4,2048]{3,2,1,0:T(4,128)(2,1)S(1)} collective-permute-done((bf16[1,2,4,2048]{3,2,1,0:T(4,128)(2,1)S(1)}, bf16[1,2,4,2048]{3,2,1,0:T(4,128)(2,1)S(1)}, u32[]{:S(2)}, u32[]{:S(2)}) %collective-permute-start.13) | collective-permute-done | bytes 32800 | tf_op jit(solution)/shard_map/ppermute | solution.py:29
  27.3 3.4 %collective-permute-done.14 = bf16[1,2,4,2048]{3,2,1,0:T(4,128)(2,1)S(1)} collective-permute-done((bf16[1,2,4,2048]{3,2,1,0:T(4,128)(2,1)S(1)}, bf16[1,2,4,2048]{3,2,1,0:T(4,128)(2,1)S(1)}, u32[]{:S(2)}, u32[]{:S(2)}) %collective-permute-start.14) | collective-permute-done | bytes 32800 | tf_op jit(solution)/shard_map/ppermute | solution.py:29
  30.8 1.0 %gather_fusion = bf16[16,2,4,2048]{3,2,1,0:T(4,128)(2,1)S(1)} fusion(bf16[16,2,4,2048]{3,2,1,0:T(4,128)(2,1)S(1)} %bitcast.91, s32[1024]{0:T(1024)S(1)} %pad_clamp_fusion.2), kind=kCustom, calls=%fused_computation.2 | custom fusion | bytes 1048640 | tf_op jit(solution)/shard_map/gather | solution.py:30
  31.8 3.6 %gather_fusion.1 = bf16[64,2,4,2048]{3,2,1,0:T(4,128)(2,1)} fusion(bf16[16,2,4,2048]{3,2,1,0:T(4,128)(2,1)S(1)} %gather_fusion, s32[1024]{0:T(1024)S(1)} %get-tuple-element.31), kind=kCustom, calls=%fused_computation.clone | custom fusion | bytes 4194560 | tf_op jit(solution)/shard_map/jit(_take)/gather | solution.py:58
  35.4 2.4 %gather_fusion.2 = bf16[64,2,4,2048]{3,2,1,0:T(4,128)(2,1)S(1)} fusion(bf16[16,2,4,2048]{3,2,1,0:T(4,128)(2,1)S(1)} %gather_fusion, s32[1024]{0:T(1024)S(1)} %get-tuple-element.30), kind=kCustom, calls=%fused_computation.1.clone | custom fusion | bytes 4194560 | tf_op jit(solution)/shard_map/jit(_take)/gather | solution.py:59
  37.7 4.0 %fusion.1 = f32[64,2,4,2048]{3,0,2,1:T(8,128)S(1)} fusion(bf16[64,2,4,2048]{3,2,1,0:T(4,128)(2,1)} %gather_fusion.1, pred[64]{0:T(512)(128)(4,1)S(1)} %get-tuple-element.6), kind=kLoop, calls=%fused_computation.7 | loop fusion | flops 2097152 | bytes 6291520 | tf_op jit(solution)/shard_map/convert_element_type | solution.py:35
  41.8 2.4 %fusion = f32[64,2,4,2048]{3,0,2,1:T(8,128)S(1)} fusion(bf16[64,2,4,2048]{3,2,1,0:T(4,128)(2,1)S(1)} %gather_fusion.2, pred[64]{0:T(512)(128)(4,1)S(1)} %get-tuple-element.28), kind=kLoop, calls=%fused_computation.5 | loop fusion | flops 2097152 | bytes 6291520 | tf_op jit(solution)/shard_map/convert_element_type | solution.py:36
  44.2 1.6 %subtract_bitcast_fusion = (f32[1,64,4,2048]{3,1,2,0:T(8,128)S(1)}, f32[1,64,4,2048]{3,1,2,0:T(8,128)S(1)}, f32[1,64,4,2048]{3,1,2,0:T(8,128)S(1)}) fusion(f32[64,2,4,2048]{3,0,2,1:T(8,128)S(1)} %fusion, f32[64,2,4,2048]{3,0,2,1:T(8,128)S(1)} %fusion.1), kind=kLoop, calls=%fused_computation.10 | loop fusion | flops 4718592 | bytes 14680064 | tf_op jit(solution)/shard_map/sub | solution.py:37
  45.8 0.7 %maximum_reduce_fusion = f32[3,64,2048]{2,1,0:T(8,128)S(1)} fusion(f32[1,64,4,2048]{3,1,2,0:T(8,128)S(1)} %get-tuple-element.12, f32[1,64,4,2048]{3,1,2,0:T(8,128)S(1)} %get-tuple-element.11, f32[1,64,4,2048]{3,1,2,0:T(8,128)S(1)} %get-tuple-element.10), kind=kLoop, calls=%fused_computation.3 | loop fusion | flops 4325376 | bytes 7864320 | tf_op jit(solution)/shard_map/reduce_sum | solution.py:42
  46.5 1.0 %fusion.3 = f32[3,64,128]{2,1,0:T(8,128)S(1)} fusion(f32[3,64,2048]{2,1,0:T(8,128)S(1)} %maximum_reduce_fusion, s32[2048]{0:T(1024)S(1)} %add_select_fusion), kind=kOutput, calls=%fused_computation.14 | convolution fusion | flops 604241920 | bytes 1679360 | tf_op jit(solution)/shard_map/dot_general | solution.py:46
  47.5 0.0 copy-done
  47.5 0.1 convolution_bitcast_fusion
  47.7 0.6 %copy.15 = f32[15,1,128]{2,1,0:T(1,128)} copy(f32[15,1,128]{2,0,1:T(8,128)S(1)} %convolution_bitcast_fusion) | data formatting | bytes 15360 | tf_op jit(solution)/shard_map/sp,pxy->sxy/dot_general | solution.py:51
  (21 shorter events, 0.4 us)
Async XLA Ops:
  0.0 47.5 %copy-start = (bf16[15,64]{1,0:T(8,128)(2,1)S(1)}, bf16[15,64]{1,0:T(8,128)(2,1)}, u32[]{:S(2)}) copy-start(bf16[15,64]{1,0:T(8,128)(2,1)} %param.7) | copy-start | bytes 5764
  0.0 6.7 %copy-start.1 = (s32[64,2]{0,1:T(2,128)S(1)}, s32[64,2]{0,1:T(2,128)}, u32[]{:S(2)}) copy-start(s32[64,2]{0,1:T(2,128)} %param.6) | copy-start | bytes 1540
  1.6 5.1 %collective-permute-start = (bf16[1,2,4,2048]{3,2,1,0:T(4,128)(2,1)S(1)}, bf16[1,2,4,2048]{3,2,1,0:T(4,128)(2,1)S(1)}, u32[]{:S(2)}, u32[]{:S(2)}) collective-permute-start(bf16[1,2,4,2048]{3,2,1,0:T(4,128)(2,1)S(1)} %get-tuple-element.27), channel_id=1, source_target_pairs={{0,1},{1,0},{2,3},{3,2},{4,5},{5,4},{6,7},{7,6},{8,9},{9,8},{10,11... | collective-permute-start | bytes 98312 | tf_op jit(solution)/shard_map/ppermute | solution.py:29
  2.2 7.3 %collective-permute-start.1 = (bf16[1,2,4,2048]{3,2,1,0:T(4,128)(2,1)S(1)}, bf16[1,2,4,2048]{3,2,1,0:T(4,128)(2,1)S(1)}, u32[]{:S(2)}, u32[]{:S(2)}) collective-permute-start(bf16[1,2,4,2048]{3,2,1,0:T(4,128)(2,1)S(1)} %get-tuple-element.26), channel_id=1, source_target_pairs={{0,2},{1,3},{2,0},{3,1},{4,6},{5,7},{6,4},{7,5},{8,10},{9,11},{10,... | collective-permute-start | bytes 98312 | tf_op jit(solution)/shard_map/ppermute | solution.py:29
  4.8 4.8 %collective-permute-start.2 = (bf16[1,2,4,2048]{3,2,1,0:T(4,128)(2,1)S(1)}, bf16[1,2,4,2048]{3,2,1,0:T(4,128)(2,1)S(1)}, u32[]{:S(2)}, u32[]{:S(2)}) collective-permute-start(bf16[1,2,4,2048]{3,2,1,0:T(4,128)(2,1)S(1)} %get-tuple-element.25), channel_id=1, source_target_pairs={{0,3},{1,2},{2,1},{3,0},{4,7},{5,6},{6,5},{7,4},{8,11},{9,10},{10,... | collective-permute-start | bytes 98312 | tf_op jit(solution)/shard_map/ppermute | solution.py:29
  4.8 7.6 %collective-permute-start.3 = (bf16[1,2,4,2048]{3,2,1,0:T(4,128)(2,1)S(1)}, bf16[1,2,4,2048]{3,2,1,0:T(4,128)(2,1)S(1)}, u32[]{:S(2)}, u32[]{:S(2)}) collective-permute-start(bf16[1,2,4,2048]{3,2,1,0:T(4,128)(2,1)S(1)} %get-tuple-element.24), channel_id=1, source_target_pairs={{0,4},{1,5},{2,6},{3,7},{4,0},{5,1},{6,2},{7,3},{8,12},{9,13},{10,... | collective-permute-start | bytes 98312 | tf_op jit(solution)/shard_map/ppermute | solution.py:29
  6.6 6.0 %collective-permute-start.4 = (bf16[1,2,4,2048]{3,2,1,0:T(4,128)(2,1)S(1)}, bf16[1,2,4,2048]{3,2,1,0:T(4,128)(2,1)S(1)}, u32[]{:S(2)}, u32[]{:S(2)}) collective-permute-start(bf16[1,2,4,2048]{3,2,1,0:T(4,128)(2,1)S(1)} %get-tuple-element.23), channel_id=1, source_target_pairs={{0,5},{1,4},{2,7},{3,6},{4,1},{5,0},{6,3},{7,2},{8,13},{9,12},{10,... | collective-permute-start | bytes 98312 | tf_op jit(solution)/shard_map/ppermute | solution.py:29
  6.7 9.4 %collective-permute-start.5 = (bf16[1,2,4,2048]{3,2,1,0:T(4,128)(2,1)S(1)}, bf16[1,2,4,2048]{3,2,1,0:T(4,128)(2,1)S(1)}, u32[]{:S(2)}, u32[]{:S(2)}) collective-permute-start(bf16[1,2,4,2048]{3,2,1,0:T(4,128)(2,1)S(1)} %get-tuple-element.22), channel_id=1, source_target_pairs={{0,6},{1,7},{2,4},{3,5},{4,2},{5,3},{6,0},{7,1},{8,14},{9,15},{10,... | collective-permute-start | bytes 98312 | tf_op jit(solution)/shard_map/ppermute | solution.py:29
  9.5 6.8 %collective-permute-start.6 = (bf16[1,2,4,2048]{3,2,1,0:T(4,128)(2,1)S(1)}, bf16[1,2,4,2048]{3,2,1,0:T(4,128)(2,1)S(1)}, u32[]{:S(2)}, u32[]{:S(2)}) collective-permute-start(bf16[1,2,4,2048]{3,2,1,0:T(4,128)(2,1)S(1)} %get-tuple-element.21), channel_id=1, source_target_pairs={{0,7},{1,6},{2,5},{3,4},{4,3},{5,2},{6,1},{7,0},{8,15},{9,14},{10,... | collective-permute-start | bytes 98312 | tf_op jit(solution)/shard_map/ppermute | solution.py:29
  9.6 10.4 %collective-permute-start.7 = (bf16[1,2,4,2048]{3,2,1,0:T(4,128)(2,1)S(1)}, bf16[1,2,4,2048]{3,2,1,0:T(4,128)(2,1)S(1)}, u32[]{:S(2)}, u32[]{:S(2)}) collective-permute-start(bf16[1,2,4,2048]{3,2,1,0:T(4,128)(2,1)S(1)} %get-tuple-element.20), channel_id=1, source_target_pairs={{0,8},{1,9},{2,10},{3,11},{4,12},{5,13},{6,14},{7,15},{8,0},{9,1},... | collective-permute-start | bytes 98312 | tf_op jit(solution)/shard_map/ppermute | solution.py:29
  12.4 7.7 %collective-permute-start.8 = (bf16[1,2,4,2048]{3,2,1,0:T(4,128)(2,1)S(1)}, bf16[1,2,4,2048]{3,2,1,0:T(4,128)(2,1)S(1)}, u32[]{:S(2)}, u32[]{:S(2)}) collective-permute-start(bf16[1,2,4,2048]{3,2,1,0:T(4,128)(2,1)S(1)} %get-tuple-element.19), channel_id=1, source_target_pairs={{0,9},{1,8},{2,11},{3,10},{4,13},{5,12},{6,15},{7,14},{8,1},{9,0},... | collective-permute-start | bytes 98312 | tf_op jit(solution)/shard_map/ppermute | solution.py:29
  12.6 12.1 %collective-permute-start.9 = (bf16[1,2,4,2048]{3,2,1,0:T(4,128)(2,1)S(1)}, bf16[1,2,4,2048]{3,2,1,0:T(4,128)(2,1)S(1)}, u32[]{:S(2)}, u32[]{:S(2)}) collective-permute-start(bf16[1,2,4,2048]{3,2,1,0:T(4,128)(2,1)S(1)} %get-tuple-element.18), channel_id=1, source_target_pairs={{0,10},{1,11},{2,8},{3,9},{4,14},{5,15},{6,12},{7,13},{8,2},{9,3},... | collective-permute-start | bytes 98312 | tf_op jit(solution)/shard_map/ppermute | solution.py:29
  16.2 8.6 %collective-permute-start.10 = (bf16[1,2,4,2048]{3,2,1,0:T(4,128)(2,1)S(1)}, bf16[1,2,4,2048]{3,2,1,0:T(4,128)(2,1)S(1)}, u32[]{:S(2)}, u32[]{:S(2)}) collective-permute-start(bf16[1,2,4,2048]{3,2,1,0:T(4,128)(2,1)S(1)} %get-tuple-element.17), channel_id=1, source_target_pairs={{0,11},{1,10},{2,9},{3,8},{4,15},{5,14},{6,13},{7,12},{8,3},{9,2},... | collective-permute-start | bytes 98312 | tf_op jit(solution)/shard_map/ppermute | solution.py:29
  16.3 8.5 %collective-permute-start.11 = (bf16[1,2,4,2048]{3,2,1,0:T(4,128)(2,1)S(1)}, bf16[1,2,4,2048]{3,2,1,0:T(4,128)(2,1)S(1)}, u32[]{:S(2)}, u32[]{:S(2)}) collective-permute-start(bf16[1,2,4,2048]{3,2,1,0:T(4,128)(2,1)S(1)} %get-tuple-element.16), channel_id=1, source_target_pairs={{0,12},{1,13},{2,14},{3,15},{4,8},{5,9},{6,10},{7,11},{8,4},{9,5},... | collective-permute-start | bytes 98312 | tf_op jit(solution)/shard_map/ppermute | solution.py:29
  20.0 5.3 %collective-permute-start.12 = (bf16[1,2,4,2048]{3,2,1,0:T(4,128)(2,1)S(1)}, bf16[1,2,4,2048]{3,2,1,0:T(4,128)(2,1)S(1)}, u32[]{:S(2)}, u32[]{:S(2)}) collective-permute-start(bf16[1,2,4,2048]{3,2,1,0:T(4,128)(2,1)S(1)} %get-tuple-element.15), channel_id=1, source_target_pairs={{0,13},{1,12},{2,15},{3,14},{4,9},{5,8},{6,11},{7,10},{8,5},{9,4},... | collective-permute-start | bytes 98312 | tf_op jit(solution)/shard_map/ppermute | solution.py:29
  20.1 7.2 %collective-permute-start.13 = (bf16[1,2,4,2048]{3,2,1,0:T(4,128)(2,1)S(1)}, bf16[1,2,4,2048]{3,2,1,0:T(4,128)(2,1)S(1)}, u32[]{:S(2)}, u32[]{:S(2)}) collective-permute-start(bf16[1,2,4,2048]{3,2,1,0:T(4,128)(2,1)S(1)} %get-tuple-element.14), channel_id=1, source_target_pairs={{0,14},{1,15},{2,12},{3,13},{4,10},{5,11},{6,8},{7,9},{8,6},{9,7},... | collective-permute-start | bytes 98312 | tf_op jit(solution)/shard_map/ppermute | solution.py:29
  24.7 6.1 %collective-permute-start.14 = (bf16[1,2,4,2048]{3,2,1,0:T(4,128)(2,1)S(1)}, bf16[1,2,4,2048]{3,2,1,0:T(4,128)(2,1)S(1)}, u32[]{:S(2)}, u32[]{:S(2)}) collective-permute-start(bf16[1,2,4,2048]{3,2,1,0:T(4,128)(2,1)S(1)} %get-tuple-element.13), channel_id=1, source_target_pairs={{0,15},{1,14},{2,13},{3,12},{4,11},{5,10},{6,9},{7,8},{8,7},{9,6},... | collective-permute-start | bytes 98312 | tf_op jit(solution)/shard_map/ppermute | solution.py:29
